TPU v7x, 256 devices: a whole 4x4x8 slice. The times are simulated.
256 devices in a mesh: rep: 8 (over x, core), seq: 32 (over y, z).
Axes of the slice: x: 4, y: 4, z: 8, core: 2. Of those that a mesh axis runs over, the one named last changes fastest.
Arguments:
- tokens: bfloat16 [16, 256, 32, 1024], P('rep', 'seq'), may hold values from -250 to 250
- cotangent: bfloat16 [16, 256, 32, 1024], P('rep', 'seq'), may hold values from -6 to 6
- clip_counts: int32 [8], P('rep'), may hold values from 1 to 2, as said below
- windows: int32 [16, 4, 3], P('rep'), may hold values from 0 to 3, as said below
- window_counts: int32 [16, 4], P('rep'), may hold values from 1 to 3, as said below
- norm_gain: float32 [1024], replicated, may hold values from 0.5 to 4
- norm_bias: float32 [1024], replicated, may hold values from -3 to 3
- qkv_weight: bfloat16 [1024, 3072], replicated, may hold values from -0.5 to 0.5
- out_weight: bfloat16 [1024, 1024], replicated, may hold values from -0.1875 to 0.1875
Outputs:
- grad_input: bfloat16 [16, 256, 32, 1024], P('rep', 'seq')
- grad_qkv_weight: float32 [1024, 3072], P('seq')
- grad_out_weight: float32 [1024, 1024], P('seq')
- grad_gain: float32 [1024], P('seq')
- grad_bias: float32 [1024], P('seq')
Inputs may be any that keep to these rules, and one draw needn't show every extreme that they name: `clip_counts`: slots of a group at or past its count hold no clip; some group is full. `windows`: the first entry of each list is the window itself; the entries of a list are distinct. `window_counts`: some window of every clip uses all 3 entries.
All inputs are finite; a program needn't handle non-finite values.
Results may differ from a plain program's by a relative error of at most 0.025.
The roundings to bfloat16 on the way count: a program that leaves them out, or rounds other values in their place, can miss the bound.
Values may be sent and summed in bfloat16 or wider, within the bound.
No kernel may reach another device: no remote copies, remote signals or barrier semaphores. Data moves between devices by JAX's collectives and lax.ppermute only.
A program may use at most 128 MiB of HBM per device.

v0:
```python
from functools import partial
import math
import jax
import jax.numpy as jnp
from jax import lax
from jax.sharding import Mesh, PartitionSpec as P
import numpy as np

D = 1024
HEADS = 16
HEAD_DIM = 64
WIN = 64
MAXW = 3
NWIN = 4
EPSILON = 1e-05


def frame_mask(window_list, list_count, frame_count):
    used_slot = jnp.arange(MAXW)[None, :] < list_count[:, None]
    listed = (window_list[:, :, None] == jnp.arange(NWIN)[None, None, :]) & used_slot[:, :, None]
    allowed = jnp.any(listed, axis=1).astype(jnp.float32)
    member = (jnp.arange(frame_count)[:, None] // WIN == jnp.arange(NWIN)[None, :]).astype(
        jnp.float32
    )
    return jnp.dot(jnp.dot(member, allowed), member.T) > 0.5


def contract_rows(left_side, right_side):
    return lax.dot_general(
        left_side, right_side, (((0,), (0,)), ((), ())), preferred_element_type=jnp.float32
    )


def times_transpose(left_side, right_side):
    return lax.dot_general(
        left_side, right_side, (((1,), (1,)), ((), ())), preferred_element_type=jnp.float32
    )


def local(
    tokens,
    cotangent,
    clip_counts,
    windows,
    window_counts,
    norm_gain,
    norm_bias,
    qkv_weight,
    out_weight,
):
    seq_size = lax.axis_size(("y", "z"))
    rep_size = lax.axis_size(("x", "core"))
    clip_count = tokens.shape[0]
    live_slot = jnp.arange(clip_count) < clip_counts[0]
    grad_live = jnp.where(live_slot[:, None, None, None], cotangent, jnp.zeros_like(cotangent))
    gathered, grad_whole = (
        lax.all_to_all(tokens, ("y", "z"), split_axis=2, concat_axis=1, tiled=True),
        lax.all_to_all(grad_live, ("y", "z"), split_axis=2, concat_axis=1, tiled=True),
    )
    frame_count = gathered.shape[1]
    patch_count = gathered.shape[2]
    row_count = clip_count * frame_count * patch_count
    grad_scale = 1.0 / math.sqrt(clip_count * rep_size * frame_count * patch_count * seq_size)
    factor = HEAD_DIM ** (-0.5)
    head_shape = (clip_count, frame_count, patch_count, HEADS, HEAD_DIM)
    allowed = jax.vmap(partial(frame_mask, frame_count=frame_count))(windows, window_counts)[
        :, None, None
    ]
    flat_input = gathered.reshape(row_count, D).astype(jnp.float32)
    centred = flat_input - jnp.mean(flat_input, axis=1, keepdims=True)
    inv_std = lax.rsqrt(jnp.mean(centred * centred, axis=1, keepdims=True) + EPSILON)
    normal_hat = centred * inv_std
    normed = (normal_hat * norm_gain + norm_bias).astype(jnp.bfloat16)
    projected = jnp.dot(normed, qkv_weight, preferred_element_type=jnp.float32).astype(jnp.bfloat16)
    query_heads = projected[:, :D].reshape(head_shape)
    key_heads = projected[:, D : 2 * D].reshape(head_shape)
    value_heads = projected[:, 2 * D :].reshape(head_shape)
    scores = (
        jnp.einsum("cfphd,cgphd->cphfg", query_heads, key_heads, preferred_element_type=jnp.float32)
        * factor
    )
    row_max = jnp.max(jnp.where(allowed, scores, -1e30), axis=-1, keepdims=True)
    exp_scores = jnp.where(allowed, jnp.exp(scores - row_max), 0.0)
    attn_prob = exp_scores / jnp.sum(exp_scores, axis=-1, keepdims=True)
    prob_bf = attn_prob.astype(jnp.bfloat16)
    attended = jnp.einsum(
        "cphfg,cgphd->cfphd", prob_bf, value_heads, preferred_element_type=jnp.float32
    ).astype(jnp.bfloat16)
    attn_flat = attended.reshape(row_count, D)
    grad_flat = grad_whole.reshape(row_count, D)
    grad_attn = times_transpose(grad_flat, out_weight).astype(jnp.bfloat16).reshape(head_shape)
    grad_prob = jnp.einsum(
        "cfphd,cgphd->cphfg", grad_attn, value_heads, preferred_element_type=jnp.float32
    )
    grad_scores = (
        attn_prob * (grad_prob - jnp.sum(attn_prob * grad_prob, axis=-1, keepdims=True)) * factor
    ).astype(jnp.bfloat16)
    grad_query = jnp.einsum(
        "cphfg,cgphd->cfphd", grad_scores, key_heads, preferred_element_type=jnp.float32
    ).astype(jnp.bfloat16)
    grad_keys = jnp.einsum(
        "cphfg,cfphd->cgphd", grad_scores, query_heads, preferred_element_type=jnp.float32
    ).astype(jnp.bfloat16)
    grad_values = jnp.einsum(
        "cphfg,cfphd->cgphd", prob_bf, grad_attn, preferred_element_type=jnp.float32
    ).astype(jnp.bfloat16)
    grad_rows = jnp.concatenate(
        [
            grad_query.reshape(row_count, D),
            grad_keys.reshape(row_count, D),
            grad_values.reshape(row_count, D),
        ],
        axis=1,
    )
    grad_normed = times_transpose(grad_rows, qkv_weight)
    gain_term = jnp.sum(grad_normed * normal_hat, axis=0) * grad_scale
    bias_term = jnp.sum(grad_normed, axis=0) * grad_scale
    grad_hat = grad_normed * norm_gain
    grad_norm_in = (
        inv_std
        * (
            grad_hat
            - jnp.mean(grad_hat, axis=1, keepdims=True)
            - normal_hat * jnp.mean(grad_hat * normal_hat, axis=1, keepdims=True)
        )
    ).astype(jnp.bfloat16)
    returned = lax.all_to_all(
        grad_norm_in.reshape(clip_count, frame_count, patch_count, D),
        ("y", "z"),
        split_axis=1,
        concat_axis=2,
        tiled=True,
    )
    grad_input = (grad_live.astype(jnp.float32) + returned.astype(jnp.float32)).astype(jnp.bfloat16)
    seq_index = lax.axis_index(("y", "z"))
    side_terms = lax.psum(jnp.stack([gain_term, bias_term]), ("x", "core", "y", "z"))
    side_terms = lax.dynamic_slice_in_dim(
        side_terms, seq_index * (D // seq_size), D // seq_size, axis=1
    )
    upper_rows = contract_rows(normed, grad_rows)
    lower_rows = contract_rows(attn_flat, grad_flat)
    stacked = (jnp.concatenate([upper_rows, lower_rows], axis=1) * grad_scale).astype(jnp.bfloat16)
    x_size = lax.axis_size("x")
    width = stacked.shape[1] // (2 * x_size)
    split = stacked.reshape(D, x_size, 2, width)
    core = lax.axis_index("core")
    mine = lax.dynamic_index_in_dim(split, core, axis=2, keepdims=False)
    other = lax.dynamic_index_in_dim(split, 1 - core, axis=2, keepdims=False)
    got = lax.ppermute(other, "core", [(0, 1), (1, 0)])
    merged = (mine.astype(jnp.float32) + got.astype(jnp.float32)).astype(jnp.bfloat16)
    merged = lax.psum_scatter(merged, "y", scatter_dimension=0, tiled=True)
    merged = lax.psum_scatter(merged, "z", scatter_dimension=0, tiled=True)
    merged = lax.psum_scatter(merged, "x", scatter_dimension=1, tiled=True)
    summed = lax.all_gather(
        merged.reshape(merged.shape[0], width), ("x", "core"), axis=1, tiled=True
    ).astype(jnp.float32)
    return (grad_input, summed[:, : 3 * D], summed[:, 3 * D :], side_terms[0], side_terms[1])


def fine_mesh(mesh):
    devices = np.asarray(mesh.devices)
    rep_size, seq_size = devices.shape
    y_size = len({device.coords[1] for device in devices.flat})
    return Mesh(
        devices.reshape(rep_size // 2, 2, y_size, seq_size // y_size), ("x", "core", "y", "z")
    )


def solution(mesh):
    rep, seq = (("x", "core"), ("y", "z"))
    return jax.shard_map(
        local,
        mesh=fine_mesh(mesh),
        in_specs=(
            P(rep, seq, None, None),
            P(rep, seq, None, None),
            P(rep),
            P(rep, None, None),
            P(rep, None),
            P(),
            P(),
            P(),
            P(),
        ),
        out_specs=(P(rep, seq, None, None), P(seq, None), P(seq, None), P(seq), P(seq)),
        check_vma=False,
    )
```

profile of v0, /device:TPU:1, one launch (start us, length us, event | category | flops | bytes accessed | tf_op | source)
XLA Modules:
  0.0 401.1 jit_solution(5838071315834525960)
XLA Ops:
  10.1 12.0 %all-to-all-start = ((bf16[2,8,32,1024]{3,1,0,2:T(8,128)(2,1)}), bf16[2,8,32,1024]{3,1,0,2:T(8,128)(2,1)S(1)}, u32[]{:S(2)}, u32[]{:S(2)}) async-start(bf16[2,8,32,1024]{3,1,0,2:T(8,128)(2,1)} %copy.100), calls=%async_computation | async-start | bytes 2097152 | tf_op jit(solution)/shard_map/all_to_all | solution.py:57
  26.6 20.4 %all-to-all-done = bf16[2,8,32,1024]{3,1,0,2:T(8,128)(2,1)S(1)} async-done(((bf16[2,8,32,1024]{3,1,0,2:T(8,128)(2,1)}), bf16[2,8,32,1024]{3,1,0,2:T(8,128)(2,1)S(1)}, u32[]{:S(2)}, u32[]{:S(2)}) %all-to-all-start) | async-done | bytes 1048608 | tf_op jit(solution)/shard_map/all_to_all | solution.py:57
  47.0 8.5 %all-to-all-start.1 = ((bf16[2,8,32,1024]{3,1,0,2:T(8,128)(2,1)}), bf16[2,8,32,1024]{3,1,0,2:T(8,128)(2,1)}, u32[]{:S(2)}, u32[]{:S(2)}) async-start(bf16[2,8,32,1024]{3,1,0,2:T(8,128)(2,1)} %copy.114), calls=%async_computation.1 | async-start | bytes 2097152 | tf_op jit(solution)/shard_map/all_to_all | solution.py:58
  63.7 6.9 %convolution_convert_fusion = bf16[512,3072]{1,0:T(8,128)(2,1)S(1)} fusion(bf16[512,1024]{1,0:T(8,128)(2,1)S(1)} %add_convert_fusion, bf16[1024,3072]{1,0:T(8,128)(2,1)} %param.16), kind=kOutput, calls=%fused_computation.13 | convolution fusion | flops 3222798336 | bytes 10485760 | tf_op jit(solution)/shard_map/dot_general | solution.py:74
  74.7 3.6 copy.120
  98.3 5.9 %fusion.71 = f32[2,16,256,256]{2,3,1,0:T(8,128)} fusion(bf16[2,256,16,64]{1,3,2,0:T(8,128)(2,1)S(1)} %copy.118, bf16[2,256,16,64]{1,3,2,0:T(8,128)(2,1)} %copy.119), kind=kOutput, calls=%fused_computation.88 | convolution fusion | flops 268435456 | bytes 10485760 | tf_op jit(solution)/shard_map/cfphd,cgphd->cphfg/dot_general | solution.py:92
  104.2 5.9 %fusion.70 = (f32[2,16,256]{2,1,0:T(8,128)S(1)}, f32[2,16,256,256]{2,3,1,0:T(8,128)}) fusion(pred[2,256,256]{1,2,0:T(8,128)(4,1)S(1)} %copy.110, bf16[2,256,16,64]{1,3,2,0:T(8,128)(2,1)S(1)} %copy-done.7, bf16[2,256,16,64]{1,3,2,0:T(8,128)(2,1)S(1)} %copy-done.6), kind=kOutput, calls=%fused_computation.87 | convolution fusion | flops 549454080 | bytes 10649600 | tf_op jit(solution)/shard_map/sub | solution.py:83
  110.0 14.1 %fusion.41 = bf16[2,256,1,16,64]{1,4,3,0,2:T(8,128)(2,1)} fusion(bf16[2,256,16,64]{1,3,2,0:T(8,128)(2,1)S(1)} %copy-done.6, f32[2,16,256,256]{2,3,1,0:T(8,128)} %fusion.71, f32[2,16,256,256]{2,3,1,0:T(8,128)} %get-tuple-element.32, f32[2,16,256]{2,1,0:T(8,128)S(1)} %get-tuple-element.31), kind=kOutput, calls=%fused_computation.43 | convolution fusion | flops 283648256 | bytes 18907136 | tf_op jit(solution)/shard_map/cphfg,cgphd->cfphd/dot_general | solution.py:98
  124.1 13.2 %fusion.38 = bf16[2,256,1,16,64]{1,4,3,0,2:T(8,128)(2,1)} fusion(bf16[2,256,16,64]{1,3,2,0:T(8,128)(2,1)S(1)} %copy-done.7, f32[2,16,256,256]{2,3,1,0:T(8,128)} %fusion.71, f32[2,16,256,256]{2,3,1,0:T(8,128)} %get-tuple-element.32, f32[2,16,256]{2,1,0:T(8,128)S(1)} %get-tuple-element.31), kind=kOutput, calls=%fused_computation.42 | convolution fusion | flops 283648256 | bytes 18907136 | tf_op jit(solution)/shard_map/cphfg,cfphd->cgphd/dot_general | solution.py:101
  137.3 4.9 %fusion.47 = bf16[2,256,1,16,64]{1,4,3,0,2:T(8,128)(2,1)S(1)} fusion(bf16[2,256,16,64]{1,3,2,0:T(8,128)(2,1)S(1)} %copy.118, f32[2,16,256,256]{2,3,1,0:T(8,128)} %get-tuple-element.32, f32[2,16,256]{2,1,0:T(8,128)S(1)} %get-tuple-element.31), kind=kOutput, calls=%fused_computation.45 | convolution fusion | flops 273154048 | bytes 10518528 | tf_op jit(solution)/shard_map/cphfg,cfphd->cgphd/dot_general | solution.py:104
  152.5 3.5 fusion.72
  156.0 4.4 %fusion.2 = bf16[1024,4096]{1,0:T(8,128)(2,1)} fusion(f32[1024,1024]{1,0:T(8,128)S(1)} %fusion.73, f32[1024,3072]{1,0:T(8,128)S(1)} %fusion.72), kind=kLoop, calls=%fused_computation.3 | loop fusion | flops 12582912 | bytes 25165824 | tf_op jit(solution)/shard_map/convert_element_type | solution.py:142
  160.4 14.4 %convert_element_type.146 = bf16[1024,4,2,512]{3,2,1,0:T(2,128)(2,1)} reshape(bf16[1024,4096]{1,0:T(8,128)(2,1)} %fusion.2) | data formatting | bytes 16777216 | tf_op jit(solution)/shard_map/convert_element_type | solution.py:142
  174.8 19.9 %constant_dynamic-slice_fusion.2 = (bf16[1024,4,1,512]{3,2,1,0:T(2,128)(2,1)S(1)}, bf16[1024,4,1,512]{3,2,1,0:T(2,128)(2,1)}) fusion(bf16[1024,4,2,512]{3,2,1,0:T(2,128)(2,1)} %convert_element_type.146, s32[]{:T(128)S(6)} %select_n.39, s32[]{:T(128)S(6)} %select_n.40), kind=kLoop, calls=%fused_computation.76 | loop fusion | bytes 16777224 | tf_op jit(solution)/shard_map/jit(dynamic_index_in_dim)/dynamic_slice | solution.py:147
  194.7 5.8 %copy.167 = bf16[1024,4,1,512]{3,0,1,2:T(8,128)(2,1)S(1)} copy(bf16[1024,4,1,512]{3,2,1,0:T(2,128)(2,1)} %get-tuple-element.25) | data formatting | bytes 8388608 | tf_op jit(solution)/shard_map/jit(dynamic_index_in_dim)/dynamic_slice | solution.py:148
  200.5 4.6 %collective-permute-start = (bf16[1024,4,512]{2,0,1:T(8,128)(2,1)S(1)}, bf16[1024,4,512]{2,0,1:T(8,128)(2,1)S(1)}, u32[]{:S(2)}, u32[]{:S(2)}) collective-permute-start(bf16[1024,4,512]{2,0,1:T(8,128)(2,1)S(1)} %bitcast.120), channel_id=1, source_target_pairs={{0,32},{32,0},{1,33},{33,1},{2,34},{34,2},{3,35},{35,3},{4,36},{36... | collective-permute-start | bytes 12582920 | tf_op jit(solution)/shard_map/ppermute | solution.py:149
  205.1 6.8 %collective-permute-done = bf16[1024,4,512]{2,0,1:T(8,128)(2,1)S(1)} collective-permute-done((bf16[1024,4,512]{2,0,1:T(8,128)(2,1)S(1)}, bf16[1024,4,512]{2,0,1:T(8,128)(2,1)S(1)}, u32[]{:S(2)}, u32[]{:S(2)}) %collective-permute-start) | collective-permute-done | bytes 4194336 | tf_op jit(solution)/shard_map/ppermute | solution.py:149
  213.9 6.7 %fusion.3 = bf16[1024,4,512]{2,0,1:T(8,128)(2,1)} fusion(bf16[1024,4,512]{2,0,1:T(8,128)(2,1)} %copy-done.5, bf16[1024,4,1,512]{3,2,1,0:T(2,128)(2,1)S(1)} %get-tuple-element.24), kind=kLoop, calls=%fused_computation.5 | loop fusion | flops 8388608 | bytes 12582912 | tf_op jit(solution)/shard_map/convert_element_type | solution.py:150
  222.2 9.0 %multiply_reduce_fusion.1 = (f32[1024]{0:T(1024)S(1)}, f32[512]{0:T(512)S(1)}, f32[512]{0:T(512)S(1)}, f32[1024]{0:T(1024)S(1)}, f32[512,1024]{1,0:T(8,128)}) fusion(f32[2,32,8,1,1024]{4,2,1,0,3:T(8,128)S(1)} %copy-done.2, f32[512]{0:T(512)S(1)} %div.35, f32[512]{0:T(512)S(1)} %rsqrt.12, f32[1024]{0:T(1024)S(1)} %copy-done.15, ...), kind=kOutput, calls=%fused_computation.27 | convolution fusion | flops 3225940992 | bytes 13651968 | tf_op jit(solution)/shard_map/dot_general | solution.py:35
  231.2 35.0 %reduce-scatter.4.cloned.1.call-done = bf16[256,4,512]{2,0,1:T(8,128)(2,1)} async-done(((bf16[1024,4,512]{2,0,1:T(8,128)(2,1)}), bf16[256,4,512]{2,0,1:T(8,128)(2,1)}) %reduce-scatter.4.cloned.1.call-update) | async-done | bytes 1048592 | tf_op jit(solution)/shard_map/reduce_scatter | solution.py:151
  270.6 8.2 %all-to-all-start.2 = ((bf16[2,256,1,1024]{3,0,2,1:T(2,128)(2,1)}), bf16[2,256,1,1024]{3,0,2,1:T(2,128)(2,1)}, u32[]{:S(2)}, u32[]{:S(2)}) async-start(bf16[2,256,1,1024]{3,0,2,1:T(2,128)(2,1)} %copy.129), calls=%async_computation.2 | async-start | bytes 2097152 | tf_op jit(solution)/shard_map/all_to_all | solution.py:127
  278.9 78.9 %psum.7 = f32[2,1024]{1,0:T(2,128)S(1)} all-reduce(f32[2,1024]{1,0:T(2,128)S(1)} %pad_maximum_fusion), channel_id=1, replica_groups=mesh['x'=4,'core'=2,'y'=4,'z'=8] {'x','core','y','z'}, use_global_device_ids=true, to_apply=%region_13.14 | all-reduce | flops 2048 | bytes 16384 | tf_op jit(solution)/shard_map/psum | solution.py:136
  362.0 14.8 %reduce-scatter.8.cloned.1.call-done = bf16[32,1,512]{2,0,1:T(8,128)(2,1)} async-done(((bf16[32,4,512]{2,0,1:T(8,128)(2,1)}), bf16[32,1,512]{2,0,1:T(8,128)(2,1)}) %reduce-scatter.8.cloned.1.call-update) | async-done | bytes 32784 | tf_op jit(solution)/shard_map/reduce_scatter | solution.py:153
  376.8 15.8 %all-gather = bf16[32,1,4096]{2,0,1:T(8,128)(2,1)S(1)} all-gather(bf16[32,1,512]{2,0,1:T(8,128)(2,1)} %reduce-scatter.8.cloned.1.call-done), channel_id=2, replica_groups=mesh['x'=4,'core'=2,'y'=4,'z'=8] {'x','core'}, dimensions={2}, use_global_device_ids=true | all-gather | bytes 294912 | tf_op jit(solution)/shard_map/all_gather | solution.py:154
  (108 shorter events, 62.6 us)
Async XLA Ops:
  7.2 75.8 %copy-start = (bf16[1024,1024]{1,0:T(8,128)(2,1)S(1)}, bf16[1024,1024]{1,0:T(8,128)(2,1)}, u32[]{:S(2)}) copy-start(bf16[1024,1024]{1,0:T(8,128)(2,1)} %param.17) | copy-start | bytes 6291460
  7.2 18.6 %copy-start.17 = (s32[2,4,3]{1,0,2:T(2,128)S(1)}, s32[2,4,3]{1,0,2:T(2,128)}, u32[]{:S(2)}) copy-start(s32[2,4,3]{1,0,2:T(2,128)} %param.12) | copy-start | bytes 292
  7.2 18.6 %copy-start.18 = (s32[2,4]{1,0:T(2,128)S(1)}, s32[2,4]{1,0:T(2,128)}, u32[]{:S(2)}) copy-start(s32[2,4]{1,0:T(2,128)} %param.13) | copy-start | bytes 100
  10.1 36.9 %all-to-all-start = ((bf16[2,8,32,1024]{3,1,0,2:T(8,128)(2,1)}), bf16[2,8,32,1024]{3,1,0,2:T(8,128)(2,1)S(1)}, u32[]{:S(2)}, u32[]{:S(2)}) async-start(bf16[2,8,32,1024]{3,1,0,2:T(8,128)(2,1)} %copy.100), calls=%async_computation | async-start | bytes 2097152 | tf_op jit(solution)/shard_map/all_to_all | solution.py:57
  47.0 33.6 %all-to-all-start.1 = ((bf16[2,8,32,1024]{3,1,0,2:T(8,128)(2,1)}), bf16[2,8,32,1024]{3,1,0,2:T(8,128)(2,1)}, u32[]{:S(2)}, u32[]{:S(2)}) async-start(bf16[2,8,32,1024]{3,1,0,2:T(8,128)(2,1)} %copy.114), calls=%async_computation.1 | async-start | bytes 2097152 | tf_op jit(solution)/shard_map/all_to_all | solution.py:58
  55.5 210.8 %reduce-scatter.4.cloned.1.call-start = ((), (), s32[]{:S(2)}) async-start(), calls=%async_computation.6 | async-start | bytes 5242880 | tf_op jit(solution)/shard_map/reduce_scatter | solution.py:151
  55.9 5.8 %copy-start.15 = (f32[1024]{0:T(1024)S(1)}, f32[1024]{0:T(1024)}, u32[]{:S(2)}) copy-start(f32[1024]{0:T(1024)} %param.14) | copy-start | bytes 12292
  55.9 5.8 %copy-start.16 = (f32[1024]{0:T(1024)S(1)}, f32[1024]{0:T(1024)}, u32[]{:S(2)}) copy-start(f32[1024]{0:T(1024)} %param.15) | copy-start | bytes 12292
  63.7 7.0 %copy-start.8 = (bf16[512,1024]{1,0:T(8,128)(2,1)}, bf16[512,1024]{1,0:T(8,128)(2,1)S(1)}, u32[]{:S(2)}) copy-start(bf16[512,1024]{1,0:T(8,128)(2,1)S(1)} %add_convert_fusion) | copy-start | bytes 3145732
  98.3 5.9 %copy-start.6 = (bf16[2,256,16,64]{1,3,2,0:T(8,128)(2,1)S(1)}, bf16[2,256,16,64]{1,3,2,0:T(8,128)(2,1)}, u32[]{:S(2)}) copy-start(bf16[2,256,16,64]{1,3,2,0:T(8,128)(2,1)} %copy.120) | copy-start | bytes 3145732
  98.3 5.9 %copy-start.7 = (bf16[2,256,16,64]{1,3,2,0:T(8,128)(2,1)S(1)}, bf16[2,256,16,64]{1,3,2,0:T(8,128)(2,1)}, u32[]{:S(2)}) copy-start(bf16[2,256,16,64]{1,3,2,0:T(8,128)(2,1)} %copy.112) | copy-start | bytes 3145732
  137.3 4.9 %copy-start.3 = (bf16[2,256,16,64]{1,3,2,0:T(8,128)(2,1)S(1)}, bf16[2,256,16,64]{1,3,2,0:T(8,128)(2,1)}, u32[]{:S(2)}) copy-start(bf16[2,256,16,64]{1,3,2,0:T(8,128)(2,1)} %copy.119) | copy-start | bytes 3145732
  137.3 6.1 %copy-start.19 = (f32[2,16,256,256]{2,3,1,0:T(8,128)S(1)}, f32[2,16,256,256]{2,3,1,0:T(8,128)}, u32[]{:S(2)}) copy-start(f32[2,16,256,256]{2,3,1,0:T(8,128)} %get-tuple-element.32) | copy-start | bytes 25165828
  144.6 1.4 copy-start.12
  147.3 2.7 copy-start.11
  152.5 3.5 copy-start.14
  200.5 11.4 %collective-permute-start = (bf16[1024,4,512]{2,0,1:T(8,128)(2,1)S(1)}, bf16[1024,4,512]{2,0,1:T(8,128)(2,1)S(1)}, u32[]{:S(2)}, u32[]{:S(2)}) collective-permute-start(bf16[1024,4,512]{2,0,1:T(8,128)(2,1)S(1)} %bitcast.120), channel_id=1, source_target_pairs={{0,32},{32,0},{1,33},{33,1},{2,34},{34,2},{3,35},{35,3},{4,36},{36... | collective-permute-start | bytes 12582920 | tf_op jit(solution)/shard_map/ppermute | solution.py:149
  211.9 2.0 copy-start.5
  220.6 1.6 copy-start.2
  220.6 137.8 %reduce-scatter.6.cloned.1.call-start = ((), (), s32[]{:S(2)}) async-start(), calls=%async_computation.7 | async-start | bytes 1179648 | tf_op jit(solution)/shard_map/reduce_scatter | solution.py:152
  266.3 92.2 %copy-start.4 = (bf16[2,8,32,1024]{3,2,1,0:T(8,128)(2,1)S(1)}, bf16[2,8,32,1024]{3,2,1,0:T(8,128)(2,1)}, u32[]{:S(2)}) copy-start(bf16[2,8,32,1024]{3,2,1,0:T(8,128)(2,1)} %param.10) | copy-start | bytes 3145732
  270.6 87.8 %all-to-all-start.2 = ((bf16[2,256,1,1024]{3,0,2,1:T(2,128)(2,1)}), bf16[2,256,1,1024]{3,0,2,1:T(2,128)(2,1)}, u32[]{:S(2)}, u32[]{:S(2)}) async-start(bf16[2,256,1,1024]{3,0,2,1:T(2,128)(2,1)} %copy.129), calls=%async_computation.2 | async-start | bytes 2097152 | tf_op jit(solution)/shard_map/all_to_all | solution.py:127
  278.8 115.3 %copy-start.1 = (bf16[1024,1024]{1,0:T(8,128)(2,1)S(1)}, bf16[1024,1024]{1,0:T(8,128)(2,1)}, u32[]{:S(2)}) copy-start(bf16[1024,1024]{1,0:T(8,128)(2,1)} %param.17) | copy-start | bytes 6291460
  278.8 98.0 %reduce-scatter.8.cloned.1.call-start = ((), (), s32[]{:S(2)}) async-start(), calls=%async_computation.8 | async-start | bytes 163840 | tf_op jit(solution)/shard_map/reduce_scatter | solution.py:153
  (3 other events, 3.5 us)
Sparse Core Ops, SparseCore 0:
  220.8 45.4 reduce-scatter.3
  268.8 46.9 reduce-scatter.5
  358.6 18.1 reduce-scatter.7
where the time goes:
time: 406 us; the launch traced here: 401 us
  blocking collectives  94.7 us (23%)
  local copies, waits for them, and re-layouts  89 us (22%)
  waiting for transfers between devices  79.4 us (20%)
  matrix products  67.3 us (17%)
  starting transfers between devices  33.7 us (8%)
  other arithmetic  21.7 us (5%)
  between operations  15.3 us (4%)
    psum x1, blocking collectives, local(): lax.psum(jnp.stack([gain_term, bias_term]), ('x', 'core', 'y', 'z'))  78.9 us
    reduce_scatter x1, waiting for transfers between devices, local(): merged = lax.psum_scatter(merged, 'y', scatter_dimension=0, tiled=True)  35 us
    all_to_all x1, waiting for transfers between devices, local(): lax.all_to_all(tokens, ('y', 'z'), split_axis=2, concat_axis=1, tiled=True)  20.4 us
    dynamic_slice x1, local copies, waits for them, and re-layouts, local(): mine = lax.dynamic_index_in_dim(split, core, axis=2, keepdims=False)  19.9 us
    another operation x8, local copies, waits for them, and re-layouts  19.9 us
    all_gather x1, blocking collectives, local(): lax.all_gather(merged.reshape(merged.shape[0], width), ('x', 'core'), axi...  15.8 us
    reduce_scatter x1, waiting for transfers between devices, local(): merged = lax.psum_scatter(merged, 'x', scatter_dimension=1, tiled=True)  14.8 us
    convert_element_type x1, local copies, waits for them, and re-layouts, local(): (jnp.concatenate([upper_rows, lower_rows], axis=1) * grad_scale).astype(j...  14.4 us
  transfers between devices with their start and end apart: 7, of which 5 were waited for; matrix products, arithmetic and copies ran while one was open for 11% of the time, Pallas kernels for 0%

commit v1 on v0

--- a/solution.py
+++ b/solution.py
@@ -133,7 +133,9 @@
     )
     grad_input = (grad_live.astype(jnp.float32) + returned.astype(jnp.float32)).astype(jnp.bfloat16)
     seq_index = lax.axis_index(("y", "z"))
-    side_terms = lax.psum(jnp.stack([gain_term, bias_term]), ("x", "core", "y", "z"))
+    side_terms = jnp.sum(
+        lax.all_gather(jnp.stack([gain_term, bias_term]), ("x", "core", "y", "z")), axis=0
+    )
     side_terms = lax.dynamic_slice_in_dim(
         side_terms, seq_index * (D // seq_size), D // seq_size, axis=1
     )

time: 406 us -> 408 us (level)
  waiting for transfers between devices: 79.4 us -> 159 us
  blocking collectives: 94.7 us -> 15.8 us
    psum x1 -> x0, blocking collectives: 78.9 us -> none  [local(): lax.psum(jnp.stack([gain_term, bias_term]), ('x', 'core', 'y', 'z'))]
    all_gather x0 -> x1, waiting for transfers between devices: none -> 74.1 us  [local(): lax.all_gather(jnp.stack([gain_term, bias_term]), ('x', 'core', 'y', 'z'))]
    reduce_scatter x1, waiting for transfers between devices: 14.8 us -> 19.1 us  [local(): merged = lax.psum_scatter(merged, 'x', scatter_dimension=1, tiled=True)]
  transfers between devices with their start and end apart: 7 -> 8, of which waited for: 5 -> 6; matrix products, arithmetic and copies ran while one was open for 11% -> 12% of each run, Pallas kernels for 0% -> 0%
where the time goes in v1:
time: 408 us; the launch traced here: 403 us
  waiting for transfers between devices  159 us (39%)
  local copies, waits for them, and re-layouts  88.9 us (22%)
  matrix products  67.3 us (16%)
  starting transfers between devices  30.4 us (7%)
  other arithmetic  24.6 us (6%)
  between operations  16.7 us (4%)
  blocking collectives  15.8 us (4%)
    all_gather x1, waiting for transfers between devices, local(): lax.all_gather(jnp.stack([gain_term, bias_term]), ('x', 'core', 'y', 'z'))  74.1 us
    reduce_scatter x1, waiting for transfers between devices, local(): merged = lax.psum_scatter(merged, 'y', scatter_dimension=0, tiled=True)  36.5 us
    all_to_all x1, waiting for transfers between devices, local(): lax.all_to_all(tokens, ('y', 'z'), split_axis=2, concat_axis=1, tiled=True)  20.4 us
    dynamic_slice x1, local copies, waits for them, and re-layouts, local(): mine = lax.dynamic_index_in_dim(split, core, axis=2, keepdims=False)  20 us
    another operation x8, local copies, waits for them, and re-layouts  19.9 us
    reduce_scatter x1, waiting for transfers between devices, local(): merged = lax.psum_scatter(merged, 'x', scatter_dimension=1, tiled=True)  19.1 us
    all_gather x1, blocking collectives, local(): lax.all_gather(merged.reshape(merged.shape[0], width), ('x', 'core'), axi...  15.8 us
    convert_element_type x1, local copies, waits for them, and re-layouts, local(): (jnp.concatenate([upper_rows, lower_rows], axis=1) * grad_scale).astype(j...  14.4 us
  transfers between devices with their start and end apart: 8, of which 6 were waited for; matrix products, arithmetic and copies ran while one was open for 12% of the time, Pallas kernels for 0%

profile of v1, /device:TPU:1, one launch (start us, length us, event | category | flops | bytes accessed | tf_op | source)
XLA Modules:
  0.0 403.1 jit_solution(11173302674513016705)
XLA Ops:
  11.0 12.0 %all-to-all-start = ((bf16[2,8,32,1024]{3,1,0,2:T(8,128)(2,1)}), bf16[2,8,32,1024]{3,1,0,2:T(8,128)(2,1)S(1)}, u32[]{:S(2)}, u32[]{:S(2)}) async-start(bf16[2,8,32,1024]{3,1,0,2:T(8,128)(2,1)} %copy.100), calls=%async_computation | async-start | bytes 2097152 | tf_op jit(solution)/shard_map/all_to_all | solution.py:57
  27.5 20.4 %all-to-all-done = bf16[2,8,32,1024]{3,1,0,2:T(8,128)(2,1)S(1)} async-done(((bf16[2,8,32,1024]{3,1,0,2:T(8,128)(2,1)}), bf16[2,8,32,1024]{3,1,0,2:T(8,128)(2,1)S(1)}, u32[]{:S(2)}, u32[]{:S(2)}) %all-to-all-start) | async-done | bytes 1048608 | tf_op jit(solution)/shard_map/all_to_all | solution.py:57
  47.9 8.5 %all-to-all-start.1 = ((bf16[2,8,32,1024]{3,1,0,2:T(8,128)(2,1)}), bf16[2,8,32,1024]{3,1,0,2:T(8,128)(2,1)}, u32[]{:S(2)}, u32[]{:S(2)}) async-start(bf16[2,8,32,1024]{3,1,0,2:T(8,128)(2,1)} %copy.114), calls=%async_computation.1 | async-start | bytes 2097152 | tf_op jit(solution)/shard_map/all_to_all | solution.py:58
  64.5 7.0 %convolution_convert_fusion = bf16[512,3072]{1,0:T(8,128)(2,1)S(1)} fusion(bf16[512,1024]{1,0:T(8,128)(2,1)S(1)} %add_convert_fusion, bf16[1024,3072]{1,0:T(8,128)(2,1)} %param.16), kind=kOutput, calls=%fused_computation.13 | convolution fusion | flops 3222798336 | bytes 10485760 | tf_op jit(solution)/shard_map/dot_general | solution.py:74
  75.5 3.6 copy.120
  99.1 5.9 %fusion.71 = f32[2,16,256,256]{2,3,1,0:T(8,128)} fusion(bf16[2,256,16,64]{1,3,2,0:T(8,128)(2,1)S(1)} %copy.118, bf16[2,256,16,64]{1,3,2,0:T(8,128)(2,1)} %copy.119), kind=kOutput, calls=%fused_computation.88 | convolution fusion | flops 268435456 | bytes 10485760 | tf_op jit(solution)/shard_map/cfphd,cgphd->cphfg/dot_general | solution.py:92
  105.0 5.9 %fusion.70 = (f32[2,16,256]{2,1,0:T(8,128)S(1)}, f32[2,16,256,256]{2,3,1,0:T(8,128)}) fusion(pred[2,256,256]{1,2,0:T(8,128)(4,1)S(1)} %copy.110, bf16[2,256,16,64]{1,3,2,0:T(8,128)(2,1)S(1)} %copy-done.7, bf16[2,256,16,64]{1,3,2,0:T(8,128)(2,1)S(1)} %copy-done.6), kind=kOutput, calls=%fused_computation.87 | convolution fusion | flops 549454080 | bytes 10649600 | tf_op jit(solution)/shard_map/sub | solution.py:83
  110.8 14.1 %fusion.41 = bf16[2,256,1,16,64]{1,4,3,0,2:T(8,128)(2,1)} fusion(bf16[2,256,16,64]{1,3,2,0:T(8,128)(2,1)S(1)} %copy-done.6, f32[2,16,256,256]{2,3,1,0:T(8,128)} %fusion.71, f32[2,16,256,256]{2,3,1,0:T(8,128)} %get-tuple-element.32, f32[2,16,256]{2,1,0:T(8,128)S(1)} %get-tuple-element.31), kind=kOutput, calls=%fused_computation.43 | convolution fusion | flops 283648256 | bytes 18907136 | tf_op jit(solution)/shard_map/cphfg,cgphd->cfphd/dot_general | solution.py:98
  124.9 13.2 %fusion.38 = bf16[2,256,1,16,64]{1,4,3,0,2:T(8,128)(2,1)} fusion(bf16[2,256,16,64]{1,3,2,0:T(8,128)(2,1)S(1)} %copy-done.7, f32[2,16,256,256]{2,3,1,0:T(8,128)} %fusion.71, f32[2,16,256,256]{2,3,1,0:T(8,128)} %get-tuple-element.32, f32[2,16,256]{2,1,0:T(8,128)S(1)} %get-tuple-element.31), kind=kOutput, calls=%fused_computation.42 | convolution fusion | flops 283648256 | bytes 18907136 | tf_op jit(solution)/shard_map/cphfg,cfphd->cgphd/dot_general | solution.py:101
  138.0 4.9 %fusion.47 = bf16[2,256,1,16,64]{1,4,3,0,2:T(8,128)(2,1)S(1)} fusion(bf16[2,256,16,64]{1,3,2,0:T(8,128)(2,1)S(1)} %copy.118, f32[2,16,256,256]{2,3,1,0:T(8,128)} %get-tuple-element.32, f32[2,16,256]{2,1,0:T(8,128)S(1)} %get-tuple-element.31), kind=kOutput, calls=%fused_computation.45 | convolution fusion | flops 273154048 | bytes 10518528 | tf_op jit(solution)/shard_map/cphfg,cfphd->cgphd/dot_general | solution.py:104
  153.3 3.5 fusion.72
  156.8 4.3 %fusion.2 = bf16[1024,4096]{1,0:T(8,128)(2,1)} fusion(f32[1024,1024]{1,0:T(8,128)S(1)} %fusion.73, f32[1024,3072]{1,0:T(8,128)S(1)} %fusion.72), kind=kLoop, calls=%fused_computation.3 | loop fusion | flops 12582912 | bytes 25165824 | tf_op jit(solution)/shard_map/convert_element_type | solution.py:144
  161.1 14.4 %convert_element_type.146 = bf16[1024,4,2,512]{3,2,1,0:T(2,128)(2,1)} reshape(bf16[1024,4096]{1,0:T(8,128)(2,1)} %fusion.2) | data formatting | bytes 16777216 | tf_op jit(solution)/shard_map/convert_element_type | solution.py:144
  175.5 20.0 %constant_dynamic-slice_fusion.2 = (bf16[1024,4,1,512]{3,2,1,0:T(2,128)(2,1)S(1)}, bf16[1024,4,1,512]{3,2,1,0:T(2,128)(2,1)}) fusion(bf16[1024,4,2,512]{3,2,1,0:T(2,128)(2,1)} %convert_element_type.146, s32[]{:T(128)S(6)} %select_n.39, s32[]{:T(128)S(6)} %select_n.40), kind=kLoop, calls=%fused_computation.76 | loop fusion | bytes 16777224 | tf_op jit(solution)/shard_map/jit(dynamic_index_in_dim)/dynamic_slice | solution.py:149
  195.5 5.8 %copy.167 = bf16[1024,4,1,512]{3,0,1,2:T(8,128)(2,1)S(1)} copy(bf16[1024,4,1,512]{3,2,1,0:T(2,128)(2,1)} %get-tuple-element.25) | data formatting | bytes 8388608 | tf_op jit(solution)/shard_map/jit(dynamic_index_in_dim)/dynamic_slice | solution.py:150
  201.3 4.6 %collective-permute-start = (bf16[1024,4,512]{2,0,1:T(8,128)(2,1)S(1)}, bf16[1024,4,512]{2,0,1:T(8,128)(2,1)S(1)}, u32[]{:S(2)}, u32[]{:S(2)}) collective-permute-start(bf16[1024,4,512]{2,0,1:T(8,128)(2,1)S(1)} %bitcast.122), channel_id=1, source_target_pairs={{0,32},{32,0},{1,33},{33,1},{2,34},{34,2},{3,35},{35,3},{4,36},{36... | collective-permute-start | bytes 12582920 | tf_op jit(solution)/shard_map/ppermute | solution.py:151
  205.9 6.8 %collective-permute-done = bf16[1024,4,512]{2,0,1:T(8,128)(2,1)S(1)} collective-permute-done((bf16[1024,4,512]{2,0,1:T(8,128)(2,1)S(1)}, bf16[1024,4,512]{2,0,1:T(8,128)(2,1)S(1)}, u32[]{:S(2)}, u32[]{:S(2)}) %collective-permute-start) | collective-permute-done | bytes 4194336 | tf_op jit(solution)/shard_map/ppermute | solution.py:151
  214.6 6.7 %fusion.3 = bf16[1024,4,512]{2,0,1:T(8,128)(2,1)} fusion(bf16[1024,4,512]{2,0,1:T(8,128)(2,1)} %copy-done.5, bf16[1024,4,1,512]{3,2,1,0:T(2,128)(2,1)S(1)} %get-tuple-element.24), kind=kLoop, calls=%fused_computation.5 | loop fusion | flops 8388608 | bytes 12582912 | tf_op jit(solution)/shard_map/convert_element_type | solution.py:152
  223.0 9.0 %multiply_reduce_fusion.1 = (f32[1024]{0:T(1024)S(1)}, f32[512]{0:T(512)S(1)}, f32[512]{0:T(512)S(1)}, f32[1024]{0:T(1024)S(1)}, f32[512,1024]{1,0:T(8,128)}) fusion(f32[2,32,8,1,1024]{4,2,1,0,3:T(8,128)S(1)} %copy-done.2, f32[512]{0:T(512)S(1)} %div.35, f32[512]{0:T(512)S(1)} %rsqrt.12, f32[1024]{0:T(1024)S(1)} %copy-done.15, ...), kind=kOutput, calls=%fused_computation.27 | convolution fusion | flops 3225940992 | bytes 13651968 | tf_op jit(solution)/shard_map/dot_general | solution.py:35
  237.0 4.8 %all-to-all-start.2 = ((bf16[2,256,1,1024]{3,0,2,1:T(2,128)(2,1)}), bf16[2,256,1,1024]{3,0,2,1:T(2,128)(2,1)}, u32[]{:S(2)}, u32[]{:S(2)}) async-start(bf16[2,256,1,1024]{3,0,2,1:T(2,128)(2,1)} %copy.129), calls=%async_computation.2 | async-start | bytes 2097152 | tf_op jit(solution)/shard_map/all_to_all | solution.py:127
  241.9 36.5 %reduce-scatter.4.cloned.1.call-done = bf16[256,4,512]{2,0,1:T(8,128)(2,1)} async-done(((bf16[1024,4,512]{2,0,1:T(8,128)(2,1)}), bf16[256,4,512]{2,0,1:T(8,128)(2,1)}) %reduce-scatter.4.cloned.1.call-update) | async-done | bytes 1048592 | tf_op jit(solution)/shard_map/reduce_scatter | solution.py:153
  282.2 74.1 %all-gather.5.cloned.1.call-done = f32[256,2,1024]{2,1,0:T(2,128)} async-done(((f32[1,2,1024]{2,1,0:T(2,128)}), f32[256,2,1024]{2,1,0:T(2,128)}) %all-gather.5.cloned.1.call-update) | async-done | bytes 2097168 | tf_op jit(solution)/shard_map/all_gather | solution.py:137
  359.1 19.1 %reduce-scatter.8.cloned.1.call-done = bf16[32,1,512]{2,0,1:T(8,128)(2,1)} async-done(((bf16[32,4,512]{2,0,1:T(8,128)(2,1)}), bf16[32,1,512]{2,0,1:T(8,128)(2,1)}) %reduce-scatter.8.cloned.1.call-update) | async-done | bytes 32784 | tf_op jit(solution)/shard_map/reduce_scatter | solution.py:155
  378.2 15.8 %all-gather = bf16[32,1,4096]{2,0,1:T(8,128)(2,1)S(1)} all-gather(bf16[32,1,512]{2,0,1:T(8,128)(2,1)} %reduce-scatter.8.cloned.1.call-done), channel_id=2, replica_groups=mesh['x'=4,'core'=2,'y'=4,'z'=8] {'x','core'}, dimensions={2}, use_global_device_ids=true | all-gather | bytes 294912 | tf_op jit(solution)/shard_map/all_gather | solution.py:156
  (111 shorter events, 65.6 us)
Async XLA Ops:
  8.0 75.8 %copy-start = (bf16[1024,1024]{1,0:T(8,128)(2,1)S(1)}, bf16[1024,1024]{1,0:T(8,128)(2,1)}, u32[]{:S(2)}) copy-start(bf16[1024,1024]{1,0:T(8,128)(2,1)} %param.17) | copy-start | bytes 6291460
  8.0 18.6 %copy-start.17 = (s32[2,4,3]{1,0,2:T(2,128)S(1)}, s32[2,4,3]{1,0,2:T(2,128)}, u32[]{:S(2)}) copy-start(s32[2,4,3]{1,0,2:T(2,128)} %param.12) | copy-start | bytes 292
  8.0 18.6 %copy-start.18 = (s32[2,4]{1,0:T(2,128)S(1)}, s32[2,4]{1,0:T(2,128)}, u32[]{:S(2)}) copy-start(s32[2,4]{1,0:T(2,128)} %param.13) | copy-start | bytes 100
  11.0 36.9 %all-to-all-start = ((bf16[2,8,32,1024]{3,1,0,2:T(8,128)(2,1)}), bf16[2,8,32,1024]{3,1,0,2:T(8,128)(2,1)S(1)}, u32[]{:S(2)}, u32[]{:S(2)}) async-start(bf16[2,8,32,1024]{3,1,0,2:T(8,128)(2,1)} %copy.100), calls=%async_computation | async-start | bytes 2097152 | tf_op jit(solution)/shard_map/all_to_all | solution.py:57
  47.9 33.6 %all-to-all-start.1 = ((bf16[2,8,32,1024]{3,1,0,2:T(8,128)(2,1)}), bf16[2,8,32,1024]{3,1,0,2:T(8,128)(2,1)}, u32[]{:S(2)}, u32[]{:S(2)}) async-start(bf16[2,8,32,1024]{3,1,0,2:T(8,128)(2,1)} %copy.114), calls=%async_computation.1 | async-start | bytes 2097152 | tf_op jit(solution)/shard_map/all_to_all | solution.py:58
  56.3 222.0 %reduce-scatter.4.cloned.1.call-start = ((), (), s32[]{:S(2)}) async-start(), calls=%async_computation.6 | async-start | bytes 5242880 | tf_op jit(solution)/shard_map/reduce_scatter | solution.py:153
  56.7 5.8 %copy-start.15 = (f32[1024]{0:T(1024)S(1)}, f32[1024]{0:T(1024)}, u32[]{:S(2)}) copy-start(f32[1024]{0:T(1024)} %param.14) | copy-start | bytes 12292
  56.7 5.8 %copy-start.16 = (f32[1024]{0:T(1024)S(1)}, f32[1024]{0:T(1024)}, u32[]{:S(2)}) copy-start(f32[1024]{0:T(1024)} %param.15) | copy-start | bytes 12292
  64.5 7.0 %copy-start.8 = (bf16[512,1024]{1,0:T(8,128)(2,1)}, bf16[512,1024]{1,0:T(8,128)(2,1)S(1)}, u32[]{:S(2)}) copy-start(bf16[512,1024]{1,0:T(8,128)(2,1)S(1)} %add_convert_fusion) | copy-start | bytes 3145732
  99.1 5.9 %copy-start.6 = (bf16[2,256,16,64]{1,3,2,0:T(8,128)(2,1)S(1)}, bf16[2,256,16,64]{1,3,2,0:T(8,128)(2,1)}, u32[]{:S(2)}) copy-start(bf16[2,256,16,64]{1,3,2,0:T(8,128)(2,1)} %copy.120) | copy-start | bytes 3145732
  99.1 5.9 %copy-start.7 = (bf16[2,256,16,64]{1,3,2,0:T(8,128)(2,1)S(1)}, bf16[2,256,16,64]{1,3,2,0:T(8,128)(2,1)}, u32[]{:S(2)}) copy-start(bf16[2,256,16,64]{1,3,2,0:T(8,128)(2,1)} %copy.112) | copy-start | bytes 3145732
  138.0 4.9 %copy-start.3 = (bf16[2,256,16,64]{1,3,2,0:T(8,128)(2,1)S(1)}, bf16[2,256,16,64]{1,3,2,0:T(8,128)(2,1)}, u32[]{:S(2)}) copy-start(bf16[2,256,16,64]{1,3,2,0:T(8,128)(2,1)} %copy.119) | copy-start | bytes 3145732
  138.0 6.1 %copy-start.19 = (f32[2,16,256,256]{2,3,1,0:T(8,128)S(1)}, f32[2,16,256,256]{2,3,1,0:T(8,128)}, u32[]{:S(2)}) copy-start(f32[2,16,256,256]{2,3,1,0:T(8,128)} %get-tuple-element.32) | copy-start | bytes 25165828
  148.1 2.7 copy-start.11
  153.3 3.5 copy-start.14
  201.3 11.4 %collective-permute-start = (bf16[1024,4,512]{2,0,1:T(8,128)(2,1)S(1)}, bf16[1024,4,512]{2,0,1:T(8,128)(2,1)S(1)}, u32[]{:S(2)}, u32[]{:S(2)}) collective-permute-start(bf16[1024,4,512]{2,0,1:T(8,128)(2,1)S(1)} %bitcast.122), channel_id=1, source_target_pairs={{0,32},{32,0},{1,33},{33,1},{2,34},{34,2},{3,35},{35,3},{4,36},{36... | collective-permute-start | bytes 12582920 | tf_op jit(solution)/shard_map/ppermute | solution.py:151
  212.7 2.0 copy-start.5
  221.4 1.6 copy-start.2
  221.4 134.9 %all-gather.5.cloned.1.call-start = ((), (), s32[]{:S(2)}) async-start(), calls=%async_computation.9 | async-start | bytes 2105344 | tf_op jit(solution)/shard_map/all_gather | solution.py:137
  232.6 45.8 %copy-start.4 = (bf16[2,8,32,1024]{3,2,1,0:T(8,128)(2,1)S(1)}, bf16[2,8,32,1024]{3,2,1,0:T(8,128)(2,1)}, u32[]{:S(2)}) copy-start(bf16[2,8,32,1024]{3,2,1,0:T(8,128)(2,1)} %param.10) | copy-start | bytes 3145732
  237.0 41.5 %all-to-all-start.2 = ((bf16[2,256,1,1024]{3,0,2,1:T(2,128)(2,1)}), bf16[2,256,1,1024]{3,0,2,1:T(2,128)(2,1)}, u32[]{:S(2)}, u32[]{:S(2)}) async-start(bf16[2,256,1,1024]{3,0,2,1:T(2,128)(2,1)} %copy.129), calls=%async_computation.2 | async-start | bytes 2097152 | tf_op jit(solution)/shard_map/all_to_all | solution.py:127
  241.8 116.7 %reduce-scatter.6.cloned.1.call-start = ((), (), s32[]{:S(2)}) async-start(), calls=%async_computation.7 | async-start | bytes 1179648 | tf_op jit(solution)/shard_map/reduce_scatter | solution.py:154
  278.4 99.8 %reduce-scatter.8.cloned.1.call-start = ((), (), s32[]{:S(2)}) async-start(), calls=%async_computation.8 | async-start | bytes 163840 | tf_op jit(solution)/shard_map/reduce_scatter | solution.py:155
  278.4 117.1 %copy-start.1 = (bf16[1024,1024]{1,0:T(8,128)(2,1)S(1)}, bf16[1024,1024]{1,0:T(8,128)(2,1)}, u32[]{:S(2)}) copy-start(bf16[1024,1024]{1,0:T(8,128)(2,1)} %param.17) | copy-start | bytes 6291460
  (4 other events, 4.9 us)
Sparse Core Ops, SparseCore 0:
  221.5 56.7 reduce-scatter.3
  280.9 34.5 reduce-scatter.5
  358.7 19.4 reduce-scatter.7
Sparse Core Ops, SparseCore 1:
  232.7 123.5 all-gather.4
